TPU v7x, 32 devices: a whole 2x2x4 slice. The times are simulated.
32 devices in a mesh: lat: 8 (over z, y), lon: 4 (over x, core).
Axes of the slice: x: 2, y: 2, z: 4, core: 2. Of those that a mesh axis runs over, the one named last changes fastest.
Arguments:
- fields: float32 [6, 32, 32, 4096], P(None, None, 'lat', 'lon'), may hold values from -6 to 6
- weights: float32 [16, 32, 4096], P(None, 'lat', 'lon'), may hold values from -2 to 2
- stencil: int32 [2, 32, 4096], P(None, 'lat', 'lon'), may hold values from -3 to 4095, as said below
- bands: float32 [6, 5, 32], replicated, may hold values from -3 to 3
Outputs:
- spectral_real: float32 [192, 32, 1280], P('lon', 'lat')
- spectral_imag: float32 [192, 32, 1280], P('lon', 'lat')
Inputs may be any that keep to these rules, and one draw needn't show every extreme that they name: stencil[0, i, j] lies in i - 3 to i; stencil[1, i, j] is (j - 16 + d) mod 4096 for some d of 0 to 29.
All inputs are finite; a program needn't handle non-finite values.
Results may differ from a plain program's by a relative error of at most 0.00007.
Values sent between devices are 32-bit elements; how exact they have to be, the bound alone decides.
No kernel may reach another device: no remote copies, remote signals or barrier semaphores. Data moves between devices by JAX's collectives and lax.ppermute only.
A program may use at most 128 MiB of HBM per device.

v0:
```python
import math

import jax
import jax.numpy as jnp
from jax import lax
from jax.sharding import PartitionSpec as P

RADIX = 64
NK = 1280
HALO = 16


def extended(block, sides, width, periodic):
    for axis, dim in sides:
        count = lax.axis_size(axis)
        forward = [(i, i + 1) for i in range(count - 1)]
        if periodic:
            forward.append((count - 1, 0))
        backward = [(target, source) for source, target in forward]
        low = lax.ppermute(
            lax.slice_in_dim(block, block.shape[dim] - width, None, axis=dim), axis, forward
        )
        high = lax.ppermute(lax.slice_in_dim(block, 0, width, axis=dim), axis, backward)
        block = jnp.concatenate([low, block, high], axis=dim)
    return block


def rows_rim(tile):
    return extended(tile, (("lat", 1),), 3, False)


def columns_rim(tile):
    return extended(tile, (("lon", 2),), HALO, True)


def spectrum(block):
    n_items, n_lines, line_len = block.shape
    highest = lax.Precision.HIGHEST
    folded = block.reshape(n_items * n_lines, RADIX, RADIX)
    digits = jnp.arange(RADIX, dtype=jnp.int32)
    angle_one = (
        2.0 * math.pi / RADIX * (digits[:, None] * digits[None, :] % RADIX).astype(jnp.float32)
    )
    first_table = jnp.concatenate([jnp.cos(angle_one), -jnp.sin(angle_one)], axis=1)
    partial_value = jnp.einsum("rab,ac->rbc", folded, first_table, precision=highest)
    angle_two = (
        2.0
        * math.pi
        / line_len
        * (digits[:, None] * digits[None, :] % line_len).astype(jnp.float32)
    )
    cos_two = jnp.cos(angle_two)
    sin_two = jnp.sin(angle_two)
    part_re = partial_value[..., :RADIX]
    part_im = partial_value[..., RADIX:]
    twisted = jnp.concatenate(
        [part_re * cos_two + part_im * sin_two, part_im * cos_two - part_re * sin_two], axis=-1
    )
    quotients = jnp.arange(NK // RADIX, dtype=jnp.int32)
    angle_three = (
        2.0 * math.pi / RADIX * (digits[:, None] * quotients[None, :] % RADIX).astype(jnp.float32)
    )
    with_cos = jnp.einsum("rbc,bq->rqc", twisted, jnp.cos(angle_three), precision=highest)
    with_sin = jnp.einsum("rbc,bq->rqc", twisted, jnp.sin(angle_three), precision=highest)
    scale = 1.0 / math.sqrt(line_len)
    real_part = (with_cos[..., :RADIX] + with_sin[..., RADIX:]) * scale
    imag_part = (with_cos[..., RADIX:] - with_sin[..., :RADIX]) * scale
    return (real_part.reshape(n_items, n_lines, NK), imag_part.reshape(n_items, n_lines, NK))


def on_device(fields, weights, stencil, bands):
    n_fields, n_levels, lat_rows, lon_cols = fields.shape
    n_items = n_fields * n_levels
    tile = fields.reshape(n_items, lat_rows, lon_cols)
    haloed = columns_rim(rows_rim(tile))
    span = lon_cols + 2 * HALO
    packed = haloed.reshape(n_items, (lat_rows + 6) * span)
    lat_start = lax.axis_index("lat") * lat_rows
    lon_start = lax.axis_index("lon") * lon_cols
    line_len = lon_cols * lax.axis_size("lon")
    local_row = (stencil[0] - lat_start + 3).reshape(-1)
    local_col = (stencil[1] - lon_start + HALO).reshape(-1)
    terms = []
    for offset_a in range(4):
        for offset_b in range(4):
            where_at = (local_row + offset_a) * span + (local_col + offset_b) % line_len
            terms.append(
                weights[4 * offset_a + offset_b].reshape(1, -1) * jnp.take(packed, where_at, axis=1)
            )
    total = terms[0]
    for term in terms[1:]:
        total = total + term
    level_major = total.reshape(n_fields, n_levels, lat_rows * lon_cols)
    stacked = jnp.pad(level_major, ((0, 0), (2, 2), (0, 0)))
    mixed = bands[:, 0, :, None] * stacked[:, 0:n_levels]
    for shift_k in range(1, 5):
        mixed = mixed + bands[:, shift_k, :, None] * stacked[:, shift_k : shift_k + n_levels]
    tiled = mixed.reshape(n_items, lat_rows, lon_cols)
    real_part, imag_part = spectrum(
        lax.all_to_all(tiled, "lon", split_axis=0, concat_axis=2, tiled=True)
    )
    return (real_part, imag_part)


def solution(mesh):
    placed = (P(None, None, "lat", "lon"), P(None, "lat", "lon"), P(None, "lat", "lon"), P())
    return jax.shard_map(
        on_device,
        mesh=mesh,
        in_specs=placed,
        out_specs=(P("lon", "lat", None), P("lon", "lat", None)),
        check_vma=False,
    )
```

profile of v0, /device:TPU:24, one launch (start us, length us, event | category | flops | bytes accessed | tf_op | source)
XLA Modules:
  0.0 596.1 jit_solution(9157800121393347588)
XLA Ops:
  0.6 3.7 copy.22
  4.4 2.7 fusion.74
  7.1 3.4 collective-permute-start
  10.5 3.3 collective-permute-start.1
  15.1 0.6 copy_bitcast_fusion.12
  16.4 0.8 multiply_bitcast_fusion.3
  17.1 0.7 compare_and_fusion.15
  18.0 45.2 %collective-permute-done = f32[192,3,1024]{2,0,1:T(8,128)} collective-permute-done((f32[192,3,1024]{2,0,1:T(8,128)}, f32[192,3,1024]{2,0,1:T(8,128)}, u32[]{:S(2)}, u32[]{:S(2)}) %collective-permute-start) | collective-permute-done | bytes 2359328 | tf_op jit(solution)/shard_map/ppermute | solution.py:20
  63.3 50.5 %collective-permute-done.1 = f32[192,3,1024]{2,0,1:T(8,128)} collective-permute-done((f32[192,3,1024]{2,0,1:T(8,128)}, f32[192,3,1024]{2,0,1:T(8,128)}, u32[]{:S(2)}, u32[]{:S(2)}) %collective-permute-start.1) | collective-permute-done | bytes 2359328 | tf_op jit(solution)/shard_map/ppermute | solution.py:23
  113.7 2.6 pad_maximum_fusion
  116.4 3.1 copy-done
  120.6 1.9 collective-permute-start.3
  122.6 0.6 slice_bitcast_fusion.20
  123.2 1.8 collective-permute-done.2
  126.1 10.9 %concatenate.13 = f32[192,10,1056]{2,0,1:T(8,128)} concatenate(f32[192,10,16]{2,0,1:T(8,128)S(1)} %copy.25, f32[192,10,1024]{2,0,1:T(8,128)} %copy-done, f32[192,10,16]{2,0,1:T(8,128)S(1)} %copy.26), dimensions={2} | concatenate | bytes 16220160 | tf_op jit(solution)/shard_map/concatenate | solution.py:24
  137.0 11.9 %copy.27 = f32[192,10,1056]{0,2,1:T(8,128)} copy(f32[192,10,1056]{2,0,1:T(8,128)} %concatenate.13) | data formatting | bytes 16220160 | tf_op jit(solution)/shard_map/concatenate | solution.py:24
  148.9 20.1 %gather_fusion = f32[4096,192]{1,0:T(8,128)} fusion(f32[192,10560]{0,1:T(8,128)} %bitcast.398, s32[4096]{0:T(1024)S(1)} %get-tuple-element.56), kind=kCustom, calls=%fused_computation.clone | custom fusion | bytes 6307840 | tf_op jit(solution)/shard_map/jit(_take)/gather | solution.py:88
  169.0 20.2 %gather_fusion.1 = f32[4096,192]{1,0:T(8,128)} fusion(f32[192,10560]{0,1:T(8,128)} %bitcast.399, s32[4096]{0:T(1024)S(1)} %get-tuple-element.64), kind=kCustom, calls=%fused_computation.1.clone | custom fusion | bytes 6307840 | tf_op jit(solution)/shard_map/jit(_take)/gather | solution.py:88
  189.2 20.2 %gather_fusion.2 = f32[4096,192]{1,0:T(8,128)} fusion(f32[192,10560]{0,1:T(8,128)} %bitcast.400, s32[4096]{0:T(1024)S(1)} %get-tuple-element.71), kind=kCustom, calls=%fused_computation.2.clone | custom fusion | bytes 6307840 | tf_op jit(solution)/shard_map/jit(_take)/gather | solution.py:88
  209.4 20.2 %gather_fusion.3 = f32[4096,192]{1,0:T(8,128)} fusion(f32[192,10560]{0,1:T(8,128)} %bitcast.401, s32[4096]{0:T(1024)S(1)} %get-tuple-element.59), kind=kCustom, calls=%fused_computation.3.clone | custom fusion | bytes 6307840 | tf_op jit(solution)/shard_map/jit(_take)/gather | solution.py:88
  229.5 20.1 %gather_fusion.4 = f32[4096,192]{1,0:T(8,128)} fusion(f32[192,10560]{0,1:T(8,128)} %bitcast.402, s32[4096]{0:T(1024)S(1)} %get-tuple-element.57), kind=kCustom, calls=%fused_computation.4.clone | custom fusion | bytes 6307840 | tf_op jit(solution)/shard_map/jit(_take)/gather | solution.py:88
  249.7 20.1 %gather_fusion.5 = f32[4096,192]{1,0:T(8,128)} fusion(f32[192,10560]{0,1:T(8,128)} %bitcast.403, s32[4096]{0:T(1024)S(1)} %get-tuple-element.63), kind=kCustom, calls=%fused_computation.5.clone | custom fusion | bytes 6307840 | tf_op jit(solution)/shard_map/jit(_take)/gather | solution.py:88
  269.8 20.2 %gather_fusion.6 = f32[4096,192]{1,0:T(8,128)} fusion(f32[192,10560]{0,1:T(8,128)} %bitcast.404, s32[4096]{0:T(1024)S(1)} %get-tuple-element.70), kind=kCustom, calls=%fused_computation.6.clone | custom fusion | bytes 6307840 | tf_op jit(solution)/shard_map/jit(_take)/gather | solution.py:88
  290.0 20.2 %gather_fusion.7 = f32[4096,192]{1,0:T(8,128)} fusion(f32[192,10560]{0,1:T(8,128)} %bitcast.405, s32[4096]{0:T(1024)S(1)} %get-tuple-element.58), kind=kCustom, calls=%fused_computation.7.clone | custom fusion | bytes 6307840 | tf_op jit(solution)/shard_map/jit(_take)/gather | solution.py:88
  310.1 20.1 %gather_fusion.8 = f32[4096,192]{1,0:T(8,128)} fusion(f32[192,10560]{0,1:T(8,128)} %bitcast.406, s32[4096]{0:T(1024)S(1)} %get-tuple-element.61), kind=kCustom, calls=%fused_computation.8.clone | custom fusion | bytes 6307840 | tf_op jit(solution)/shard_map/jit(_take)/gather | solution.py:88
  330.3 20.1 %gather_fusion.9 = f32[4096,192]{1,0:T(8,128)} fusion(f32[192,10560]{0,1:T(8,128)} %bitcast.407, s32[4096]{0:T(1024)S(1)} %get-tuple-element.62), kind=kCustom, calls=%fused_computation.9.clone | custom fusion | bytes 6307840 | tf_op jit(solution)/shard_map/jit(_take)/gather | solution.py:88
  350.4 20.1 %gather_fusion.10 = f32[4096,192]{1,0:T(8,128)} fusion(f32[192,10560]{0,1:T(8,128)} %bitcast.408, s32[4096]{0:T(1024)S(1)} %get-tuple-element.69), kind=kCustom, calls=%fused_computation.10.clone | custom fusion | bytes 6307840 | tf_op jit(solution)/shard_map/jit(_take)/gather | solution.py:88
  370.6 20.2 %gather_fusion.11 = f32[4096,192]{1,0:T(8,128)} fusion(f32[192,10560]{0,1:T(8,128)} %bitcast.409, s32[4096]{0:T(1024)S(1)} %get-tuple-element.60), kind=kCustom, calls=%fused_computation.11.clone | custom fusion | bytes 6307840 | tf_op jit(solution)/shard_map/jit(_take)/gather | solution.py:88
  390.8 20.2 %gather_fusion.12 = f32[4096,192]{1,0:T(8,128)} fusion(f32[192,10560]{0,1:T(8,128)} %bitcast.410, s32[4096]{0:T(1024)S(1)} %get-tuple-element.67), kind=kCustom, calls=%fused_computation.12.clone | custom fusion | bytes 6307840 | tf_op jit(solution)/shard_map/jit(_take)/gather | solution.py:88
  410.9 20.1 %gather_fusion.13 = f32[4096,192]{1,0:T(8,128)} fusion(f32[192,10560]{0,1:T(8,128)} %bitcast.411, s32[4096]{0:T(1024)S(1)} %get-tuple-element.65), kind=kCustom, calls=%fused_computation.13.clone | custom fusion | bytes 6307840 | tf_op jit(solution)/shard_map/jit(_take)/gather | solution.py:88
  431.0 20.1 %gather_fusion.14 = f32[4096,192]{1,0:T(8,128)} fusion(f32[192,10560]{0,1:T(8,128)} %bitcast.412, s32[4096]{0:T(1024)S(1)} %get-tuple-element.68), kind=kCustom, calls=%fused_computation.14.clone | custom fusion | bytes 6307840 | tf_op jit(solution)/shard_map/jit(_take)/gather | solution.py:88
  451.4 20.2 %gather_fusion.15 = f32[4096,192]{1,0:T(8,128)} fusion(f32[192,10560]{0,1:T(8,128)} %bitcast.413, s32[4096]{0:T(1024)S(1)} %get-tuple-element.66), kind=kCustom, calls=%fused_computation.15.clone | custom fusion | bytes 6307840 | tf_op jit(solution)/shard_map/jit(_take)/gather | solution.py:88
  471.7 31.6 %fusion = f32[192,4096]{0,1:T(8,128)} fusion(f32[4096,192]{1,0:T(8,128)} %gather_fusion.15, f32[4096,192]{1,0:T(8,128)} %gather_fusion.14, f32[4096,192]{1,0:T(8,128)} %gather_fusion.13, f32[4096,192]{1,0:T(8,128)} %gather_fusion.12, f32[4096,192]{1,0:T(8,128)} %gather_fusion.11, f32[4096,192]{1,0:T(8,128)} %gather_fusion.10, f32[4096,192]{1,0:T(8,128)} %gather_fusion.9, ...), kind=kLoop, calls=%fused_computation.25 | loop fusion | flops 36962304 | bytes 53805056 | tf_op jit(solution)/shard_map/add | solution.py:92
  503.4 3.7 copy.28
  507.2 3.1 fusion.19
  510.3 5.2 reshape.123
  515.5 3.9 all-to-all-start
  519.7 36.7 %all-to-all-done = f32[192,4,1024]{2,1,0:T(4,128)S(1)} async-done(((f32[192,4,1024]{2,1,0:T(4,128)}), f32[192,4,1024]{2,1,0:T(4,128)S(1)}, u32[]{:S(2)}, u32[]{:S(2)}) %all-to-all-start) | async-done | bytes 3145760 | tf_op jit(solution)/shard_map/all_to_all | solution.py:100
  556.5 1.8 copy.29
  558.3 2.0 copy.30
  560.3 4.3 reshape.124
  564.6 12.4 %fusion.33 = f32[192,64,128]{2,1,0:T(8,128)S(1)} fusion(f32[192,64,64]{2,1,0:T(8,128)} %reshape.124, f32[64,64]{1,0:T(8,128)S(1)} %get-tuple-element.88, f32[64,64]{1,0:T(8,128)S(1)} %get-tuple-element.89), kind=kOutput, calls=%fused_computation.97 | convolution fusion | flops 1207967744 | bytes 9469952 | tf_op jit(solution)/shard_map/rab,ac->rbc/dot_general | solution.py:45
  577.0 3.3 multiply_add_fusion
  580.3 4.4 fusion.27
  584.7 4.2 fusion.28
  588.9 2.7 fusion.23
  591.6 2.9 reshape.125
  594.5 1.6 reshape.126
  (79 shorter events, 4.7 us)
Async XLA Ops:
  4.3 9.5 %copy-start.1 = (f32[16,4,1024]{2,1,0:T(4,128)S(1)}, f32[16,4,1024]{2,1,0:T(4,128)}, u32[]{:S(2)}) copy-start(f32[16,4,1024]{2,1,0:T(4,128)} %param.7) | copy-start | bytes 786436
  7.1 56.2 %collective-permute-start = (f32[192,3,1024]{2,0,1:T(8,128)}, f32[192,3,1024]{2,0,1:T(8,128)}, u32[]{:S(2)}, u32[]{:S(2)}) collective-permute-start(f32[192,3,1024]{2,0,1:T(8,128)} %get-tuple-element.9), channel_id=1, source_target_pairs={{0,4},{4,8},{8,12},{12,16},{16,20},{20,24},{24,28},{1,5},{5,9},{9,... | collective-permute-start | bytes 7077896 | tf_op jit(solution)/shard_map/ppermute | solution.py:20
  10.5 103.2 %collective-permute-start.1 = (f32[192,3,1024]{2,0,1:T(8,128)}, f32[192,3,1024]{2,0,1:T(8,128)}, u32[]{:S(2)}, u32[]{:S(2)}) collective-permute-start(f32[192,3,1024]{2,0,1:T(8,128)} %get-tuple-element.10), channel_id=1, source_target_pairs={{4,0},{8,4},{12,8},{16,12},{20,16},{24,20},{28,24},{5,1},{9,5},{13... | collective-permute-start | bytes 7077896 | tf_op jit(solution)/shard_map/ppermute | solution.py:23
  116.4 3.1 copy-start
  119.5 3.1 copy-start.9
  120.2 4.8 collective-permute-start.2
  120.6 5.1 collective-permute-start.3
  451.2 20.4 %copy-start.2 = (f32[4096]{0:T(1024)S(1)}, f32[4096]{0:T(1024)}, u32[]{:S(2)}) copy-start(f32[4096]{0:T(1024)} %get-tuple-element.81) | copy-start | bytes 49156
  451.2 20.4 %copy-start.3 = (f32[4096]{0:T(1024)S(1)}, f32[4096]{0:T(1024)}, u32[]{:S(2)}) copy-start(f32[4096]{0:T(1024)} %get-tuple-element.82) | copy-start | bytes 49156
  451.2 20.4 %copy-start.4 = (f32[4096]{0:T(1024)S(1)}, f32[4096]{0:T(1024)}, u32[]{:S(2)}) copy-start(f32[4096]{0:T(1024)} %get-tuple-element.83) | copy-start | bytes 49156
  451.2 20.4 %copy-start.5 = (f32[4096]{0:T(1024)S(1)}, f32[4096]{0:T(1024)}, u32[]{:S(2)}) copy-start(f32[4096]{0:T(1024)} %get-tuple-element.84) | copy-start | bytes 49156
  451.2 20.4 %copy-start.6 = (f32[4096]{0:T(1024)S(1)}, f32[4096]{0:T(1024)}, u32[]{:S(2)}) copy-start(f32[4096]{0:T(1024)} %get-tuple-element.85) | copy-start | bytes 49156
  451.2 20.4 %copy-start.7 = (f32[4096]{0:T(1024)S(1)}, f32[4096]{0:T(1024)}, u32[]{:S(2)}) copy-start(f32[4096]{0:T(1024)} %get-tuple-element.86) | copy-start | bytes 49156
  451.2 20.4 %copy-start.8 = (f32[4096]{0:T(1024)S(1)}, f32[4096]{0:T(1024)}, u32[]{:S(2)}) copy-start(f32[4096]{0:T(1024)} %get-tuple-element.87) | copy-start | bytes 49156
  451.2 20.4 %copy-start.10 = (pred[4096]{0:T(1024)(128)(4,1)S(1)}, pred[4096]{0:T(1024)(128)(4,1)}, u32[]{:S(2)}) copy-start(pred[4096]{0:T(1024)(128)(4,1)} %get-tuple-element.40) | copy-start | bytes 12292
  451.2 20.4 %copy-start.11 = (pred[4096]{0:T(1024)(128)(4,1)S(1)}, pred[4096]{0:T(1024)(128)(4,1)}, u32[]{:S(2)}) copy-start(pred[4096]{0:T(1024)(128)(4,1)} %get-tuple-element.41) | copy-start | bytes 12292
  451.2 20.4 %copy-start.12 = (pred[4096]{0:T(1024)(128)(4,1)S(1)}, pred[4096]{0:T(1024)(128)(4,1)}, u32[]{:S(2)}) copy-start(pred[4096]{0:T(1024)(128)(4,1)} %get-tuple-element.42) | copy-start | bytes 12292
  451.2 20.4 %copy-start.13 = (pred[4096]{0:T(1024)(128)(4,1)S(1)}, pred[4096]{0:T(1024)(128)(4,1)}, u32[]{:S(2)}) copy-start(pred[4096]{0:T(1024)(128)(4,1)} %get-tuple-element.43) | copy-start | bytes 12292
  451.2 20.4 %copy-start.14 = (pred[4096]{0:T(1024)(128)(4,1)S(1)}, pred[4096]{0:T(1024)(128)(4,1)}, u32[]{:S(2)}) copy-start(pred[4096]{0:T(1024)(128)(4,1)} %get-tuple-element.44) | copy-start | bytes 12292
  451.2 20.4 %copy-start.15 = (pred[4096]{0:T(1024)(128)(4,1)S(1)}, pred[4096]{0:T(1024)(128)(4,1)}, u32[]{:S(2)}) copy-start(pred[4096]{0:T(1024)(128)(4,1)} %get-tuple-element.45) | copy-start | bytes 12292
  451.3 20.4 %copy-start.16 = (pred[4096]{0:T(1024)(128)(4,1)S(1)}, pred[4096]{0:T(1024)(128)(4,1)}, u32[]{:S(2)}) copy-start(pred[4096]{0:T(1024)(128)(4,1)} %get-tuple-element.46) | copy-start | bytes 12292
  451.3 20.4 %copy-start.17 = (pred[4096]{0:T(1024)(128)(4,1)S(1)}, pred[4096]{0:T(1024)(128)(4,1)}, u32[]{:S(2)}) copy-start(pred[4096]{0:T(1024)(128)(4,1)} %get-tuple-element.47) | copy-start | bytes 12292
  451.3 20.4 %copy-start.18 = (pred[4096]{0:T(1024)(128)(4,1)S(1)}, pred[4096]{0:T(1024)(128)(4,1)}, u32[]{:S(2)}) copy-start(pred[4096]{0:T(1024)(128)(4,1)} %get-tuple-element.48) | copy-start | bytes 12292
  451.3 20.4 %copy-start.19 = (pred[4096]{0:T(1024)(128)(4,1)S(1)}, pred[4096]{0:T(1024)(128)(4,1)}, u32[]{:S(2)}) copy-start(pred[4096]{0:T(1024)(128)(4,1)} %get-tuple-element.49) | copy-start | bytes 12292
  451.3 20.4 %copy-start.20 = (pred[4096]{0:T(1024)(128)(4,1)S(1)}, pred[4096]{0:T(1024)(128)(4,1)}, u32[]{:S(2)}) copy-start(pred[4096]{0:T(1024)(128)(4,1)} %get-tuple-element.50) | copy-start | bytes 12292
  451.3 20.4 %copy-start.21 = (pred[4096]{0:T(1024)(128)(4,1)S(1)}, pred[4096]{0:T(1024)(128)(4,1)}, u32[]{:S(2)}) copy-start(pred[4096]{0:T(1024)(128)(4,1)} %get-tuple-element.51) | copy-start | bytes 12292
  451.3 20.4 %copy-start.22 = (pred[4096]{0:T(1024)(128)(4,1)S(1)}, pred[4096]{0:T(1024)(128)(4,1)}, u32[]{:S(2)}) copy-start(pred[4096]{0:T(1024)(128)(4,1)} %get-tuple-element.52) | copy-start | bytes 12292
  451.3 20.4 %copy-start.23 = (pred[4096]{0:T(1024)(128)(4,1)S(1)}, pred[4096]{0:T(1024)(128)(4,1)}, u32[]{:S(2)}) copy-start(pred[4096]{0:T(1024)(128)(4,1)} %get-tuple-element.53) | copy-start | bytes 12292
  451.3 20.4 %copy-start.24 = (pred[4096]{0:T(1024)(128)(4,1)S(1)}, pred[4096]{0:T(1024)(128)(4,1)}, u32[]{:S(2)}) copy-start(pred[4096]{0:T(1024)(128)(4,1)} %get-tuple-element.54) | copy-start | bytes 12292
  451.3 20.4 %copy-start.25 = (pred[4096]{0:T(1024)(128)(4,1)S(1)}, pred[4096]{0:T(1024)(128)(4,1)}, u32[]{:S(2)}) copy-start(pred[4096]{0:T(1024)(128)(4,1)} %get-tuple-element.55) | copy-start | bytes 12292
  503.3 3.8 copy-start.26
  503.3 3.8 copy-start.27
  503.3 3.8 copy-start.28
  503.3 3.8 copy-start.29
  503.4 3.8 copy-start.30
  515.5 41.0 %all-to-all-start = ((f32[192,4,1024]{2,1,0:T(4,128)}), f32[192,4,1024]{2,1,0:T(4,128)S(1)}, u32[]{:S(2)}, u32[]{:S(2)}) async-start(f32[192,4,1024]{2,1,0:T(4,128)} %reshape.123), calls=%async_computation | async-start | bytes 6291456 | tf_op jit(solution)/shard_map/all_to_all | solution.py:100
where the time goes:
time: 598 us; the launch traced here: 596 us
  local copies, waits for them, and re-layouts  381 us (64%)
  waiting for transfers between devices  135 us (23%)
  other arithmetic  45.3 us (8%)
  matrix products  21 us (4%)
  starting transfers between devices  12.6 us (2%)
    gather x16, local copies, waits for them, and re-layouts, on_device(): jnp.take(packed, where_at, axis=1)  322 us
    ppermute x2, waiting for transfers between devices, extended(): lax.ppermute(lax.slice_in_dim(block, 0, width, axis=dim), axis, backward)  50.9 us
    ppermute x2, waiting for transfers between devices, extended(): lax.ppermute(lax.slice_in_dim(block, block.shape[dim] - width, None, axis...  47 us
    all_to_all x1, waiting for transfers between devices, on_device(): lax.all_to_all(tiled, 'lon', split_axis=0, concat_axis=2, tiled=True)  36.7 us
    add x1, other arithmetic, on_device(): total = total + term  31.6 us
    concatenate x2, local copies, waits for them, and re-layouts, extended(): block = jnp.concatenate([low, block, high], axis=dim)  22.8 us
    dot_general x1, matrix products, spectrum(): jnp.einsum('rab,ac->rbc', folded, first_table, precision=highest)  12.4 us
  transfers between devices with their start and end apart: 5, of which 5 were waited for; matrix products, arithmetic and copies ran while one was open for 1% of the time, Pallas kernels for 0%

commit v1 on v0

v1 whole, which is shorter than its diff:
```python
import functools
import math

import jax
import jax.numpy as jnp
from jax import lax
from jax.experimental import pallas as pl
from jax.experimental.pallas import tpu as pltpu
from jax.sharding import PartitionSpec as P

RADIX = 64
NK = 1280
HALO = 16
ROWS_OUT = 3
TAPS = 4
LANES = 128
WINDOW = 256


def shifted(block, axis, width, dim, periodic):
    count = lax.axis_size(axis)
    forward = [(i, i + 1) for i in range(count - 1)]
    if periodic:
        forward.append((count - 1, 0))
    backward = [(target, source) for source, target in forward]
    low = lax.ppermute(
        lax.slice_in_dim(block, block.shape[dim] - width, None, axis=dim), axis, forward
    )
    high = lax.ppermute(lax.slice_in_dim(block, 0, width, axis=dim), axis, backward)
    return low, high


def spectrum(block):
    n_items, n_lines, line_len = block.shape
    highest = lax.Precision.HIGHEST
    folded = block.reshape(n_items * n_lines, RADIX, RADIX)
    digits = jnp.arange(RADIX, dtype=jnp.int32)
    angle_one = (
        2.0 * math.pi / RADIX * (digits[:, None] * digits[None, :] % RADIX).astype(jnp.float32)
    )
    first_table = jnp.concatenate([jnp.cos(angle_one), -jnp.sin(angle_one)], axis=1)
    partial_value = jnp.einsum("rab,ac->rbc", folded, first_table, precision=highest)
    angle_two = (
        2.0
        * math.pi
        / line_len
        * (digits[:, None] * digits[None, :] % line_len).astype(jnp.float32)
    )
    cos_two = jnp.cos(angle_two)
    sin_two = jnp.sin(angle_two)
    part_re = partial_value[..., :RADIX]
    part_im = partial_value[..., RADIX:]
    twisted = jnp.concatenate(
        [part_re * cos_two + part_im * sin_two, part_im * cos_two - part_re * sin_two], axis=-1
    )
    quotients = jnp.arange(NK // RADIX, dtype=jnp.int32)
    angle_three = (
        2.0 * math.pi / RADIX * (digits[:, None] * quotients[None, :] % RADIX).astype(jnp.float32)
    )
    with_cos = jnp.einsum("rbc,bq->rqc", twisted, jnp.cos(angle_three), precision=highest)
    with_sin = jnp.einsum("rbc,bq->rqc", twisted, jnp.sin(angle_three), precision=highest)
    scale = 1.0 / math.sqrt(line_len)
    real_part = (with_cos[..., :RADIX] + with_sin[..., RADIX:]) * scale
    imag_part = (with_cos[..., RADIX:] - with_sin[..., :RADIX]) * scale
    return (real_part.reshape(n_items, n_lines, NK), imag_part.reshape(n_items, n_lines, NK))


def interp_kernel(hi_ref, lo_ref, info_ref, out_ref):
    row = pl.program_id(0)
    block = pl.program_id(1)
    info = info_ref[0]
    offset_r = info[16:17, :]
    offset_d = info[17:18, :]
    c_index = lax.broadcasted_iota(jnp.int32, (WINDOW, LANES), 0).astype(jnp.float32)
    j_index = lax.broadcasted_iota(jnp.int32, (WINDOW, LANES), 1).astype(jnp.float32)
    tap = c_index - j_index - offset_d
    masks = [tap == float(b) for b in range(TAPS)]
    start = pl.multiple_of(block * LANES, LANES)
    acc = jnp.zeros(out_ref.shape[1:], jnp.float32)
    for p in range(2 * ROWS_OUT + 1):
        picked = []
        for b in range(TAPS):
            value = jnp.zeros_like(offset_r)
            for a in range(TAPS):
                if 0 <= p - a <= ROWS_OUT:
                    value = jnp.where(offset_r == float(p - a), info[4 * a + b : 4 * a + b + 1, :], value)
            picked.append(value)
        matrix = jnp.where(
            masks[0],
            picked[0],
            jnp.where(masks[1], picked[1], jnp.where(masks[2], picked[2], jnp.where(masks[3], picked[3], 0.0))),
        )
        m_hi = matrix.astype(jnp.bfloat16)
        m_lo = (matrix - m_hi.astype(jnp.float32)).astype(jnp.bfloat16)
        x_hi = hi_ref[row + p, :, pl.ds(start, WINDOW)]
        x_lo = lo_ref[row + p, :, pl.ds(start, WINDOW)]
        acc = acc + jnp.dot(x_hi, m_hi, preferred_element_type=jnp.float32)
        acc = acc + jnp.dot(x_hi, m_lo, preferred_element_type=jnp.float32)
        acc = acc + jnp.dot(x_lo, m_hi, preferred_element_type=jnp.float32)
    out_ref[0] = acc


def interpolate(x_hi, x_lo, info, lat_rows, lon_cols):
    n_rows, n_items, width = x_hi.shape
    blocks = lon_cols // LANES
    return pl.pallas_call(
        interp_kernel,
        out_shape=jax.ShapeDtypeStruct((lat_rows, n_items, lon_cols), jnp.float32),
        grid=(lat_rows, blocks),
        in_specs=[
            pl.BlockSpec((n_rows, n_items, width), lambda i, jb: (0, 0, 0)),
            pl.BlockSpec((n_rows, n_items, width), lambda i, jb: (0, 0, 0)),
            pl.BlockSpec((1, info.shape[1], LANES), lambda i, jb: (i, 0, jb)),
        ],
        out_specs=pl.BlockSpec((1, n_items, LANES), lambda i, jb: (i, 0, jb)),
        compiler_params=pltpu.CompilerParams(vmem_limit_bytes=60 * 1024 * 1024),
    )(x_hi, x_lo, info)


def on_device(fields, weights, stencil, bands):
    n_fields, n_levels, lat_rows, lon_cols = fields.shape
    n_items = n_fields * n_levels
    rows_major = jnp.transpose(fields, (2, 0, 1, 3))
    stacked = jnp.pad(rows_major, ((0, 0), (0, 0), (2, 2), (0, 0)))
    mixed = bands[None, :, 0, :, None] * stacked[:, :, 0:n_levels]
    for shift_k in range(1, 5):
        mixed = mixed + bands[None, :, shift_k, :, None] * stacked[:, :, shift_k : shift_k + n_levels]
    tile = mixed.reshape(lat_rows, n_items, lon_cols)
    left, right = shifted(tile, "lon", HALO, 2, True)
    wide = jnp.concatenate([left, tile, right], axis=2)
    below, above = shifted(wide, "lat", ROWS_OUT, 0, False)
    haloed = jnp.concatenate([below, wide, above], axis=0)
    width = lon_cols + LANES
    haloed = jnp.pad(haloed, ((0, 0), (0, 0), (0, width - haloed.shape[2])))
    rounded = lax.reduce_precision(haloed, exponent_bits=8, mantissa_bits=7)
    x_hi = rounded.astype(jnp.bfloat16)
    x_lo = (haloed - rounded).astype(jnp.bfloat16)

    lat_start = lax.axis_index("lat") * lat_rows
    lon_start = lax.axis_index("lon") * lon_cols
    line_len = lon_cols * lax.axis_size("lon")
    row_g = lat_start + jnp.arange(lat_rows, dtype=jnp.int32)[:, None]
    col_g = lon_start + jnp.arange(lon_cols, dtype=jnp.int32)[None, :]
    offset_r = (stencil[0] - row_g + ROWS_OUT).astype(jnp.float32)
    offset_d = jnp.mod(stencil[1] - col_g + HALO, line_len).astype(jnp.float32)
    info = jnp.concatenate(
        [
            jnp.transpose(weights, (1, 0, 2)),
            offset_r[:, None, :],
            offset_d[:, None, :],
            jnp.zeros((lat_rows, 6, lon_cols), jnp.float32),
        ],
        axis=1,
    )
    departed = interpolate(x_hi, x_lo, info, lat_rows, lon_cols)
    gathered = lax.all_to_all(departed, "lon", split_axis=1, concat_axis=2, tiled=True)
    lines = jnp.transpose(gathered, (1, 0, 2))
    real_part, imag_part = spectrum(lines)
    return (real_part, imag_part)


def solution(mesh):
    placed = (P(None, None, "lat", "lon"), P(None, "lat", "lon"), P(None, "lat", "lon"), P())
    return jax.shard_map(
        on_device,
        mesh=mesh,
        in_specs=placed,
        out_specs=(P("lon", "lat", None), P("lon", "lat", None)),
        check_vma=False,
    )
```

time: 598 us -> 282 us (0.47)
  local copies, waits for them, and re-layouts: 381 us -> 40.4 us
  Pallas kernels: 0 us -> 31 us
  other arithmetic: 45.3 us -> 21.8 us
  waiting for transfers between devices: 135 us -> 155 us
    gather x16 -> x0, local copies, waits for them, and re-layouts: 322 us -> none  [on_device(): jnp.take(packed, where_at, axis=1)]
    pallas_call x0 -> x1, Pallas kernels: none -> 31 us  [interpolate(): pl.pallas_call(interp_kernel, out_shape=jax.ShapeDtypeStruct((lat_rows, n...]
    add x2 -> x3, other arithmetic: 34.7 us -> 7.8 us  [the longest x1 7.79 us: on_device(): mixed + bands[None, :, shift_k, :, None] * stacked[:, :, shift_k:shift_k...]
    ppermute x4, waiting for transfers between devices: 97.9 us -> 118 us  [the longest x2 66.2 us: shifted(): lax.ppermute(lax.slice_in_dim(block, 0, width, axis=dim), axis, backward)]
    concatenate x2, local copies, waits for them, and re-layouts: 22.8 us -> 3.92 us  [the longest x1 3.84 us: on_device(): wide = jnp.concatenate([left, tile, right], axis=2)]
  transfers between devices with their start and end apart: 5 -> 5, of which waited for: 5 -> 5; matrix products, arithmetic and copies ran while one was open for 1% -> 2% of each run, Pallas kernels for 0% -> 0%
where the time goes in v1:
time: 282 us; the launch traced here: 281 us
  waiting for transfers between devices  155 us (55%)
  local copies, waits for them, and re-layouts  40.4 us (14%)
  Pallas kernels  31 us (11%)
  other arithmetic  21.8 us (8%)
  matrix products  21 us (7%)
  starting transfers between devices  11.6 us (4%)
    ppermute x2, waiting for transfers between devices, shifted(): lax.ppermute(lax.slice_in_dim(block, 0, width, axis=dim), axis, backward)  66.2 us
    ppermute x2, waiting for transfers between devices, shifted(): lax.ppermute(lax.slice_in_dim(block, block.shape[dim] - width, None, axis...  51.8 us
    all_to_all x1, waiting for transfers between devices, on_device(): lax.all_to_all(departed, 'lon', split_axis=1, concat_axis=2, tiled=True)  36.8 us
    pallas_call x1, Pallas kernels, interpolate(): pl.pallas_call(interp_kernel, out_shape=jax.ShapeDtypeStruct((lat_rows, n...  31 us
    dot_general x1, matrix products, spectrum(): jnp.einsum('rab,ac->rbc', folded, first_table, precision=highest)  12.4 us
    add x1, other arithmetic, on_device(): mixed + bands[None, :, shift_k, :, None] * stacked[:, :, shift_k:shift_k...  7.79 us
    all_to_all x2, local copies, waits for them, and re-layouts, on_device(): lax.all_to_all(departed, 'lon', split_axis=1, concat_axis=2, tiled=True)  7.58 us
    reshape x1, local copies, waits for them, and re-layouts, spectrum(): folded = block.reshape(n_items * n_lines, RADIX, RADIX)  6.37 us
  transfers between devices with their start and end apart: 5, of which 5 were waited for; matrix products, arithmetic and copies ran while one was open for 2% of the time, Pallas kernels for 0%

profile of v1, /device:TPU:24, one launch (start us, length us, event | category | flops | bytes accessed | tf_op | source)
XLA Modules:
  0.0 281.3 jit_solution(5519550791013404727)
XLA Ops:
  0.6 0.8 slice_bitcast_fusion.4
  1.4 7.8 %multiply_add_fusion.1 = f32[4,6,32,1024]{3,0,2,1:T(4,128)S(1)} fusion(f32[4,6,32,1024]{3,0,2,1:T(4,128)} %bitcast.55, f32[6,32]{1,0:T(8,128)S(1)} %get-tuple-element.17, f32[6,32]{1,0:T(8,128)S(1)} %get-tuple-element.18, f32[6,32]{1,0:T(8,128)S(1)} %get-tuple-element.15, f32[6,32]{1,0:T(8,128)S(1)} %get-tuple-element.16, f32[6,32]{1,0:T(8,128)S(1)} %get-tuple-element.14), kind=kLoop, calls=%fused_computation.10 | loop fusion | flops 7077888 | bytes 6295296 | tf_op jit(solution)/shard_map/add | solution.py:127
  9.2 1.8 copy.17
  11.0 0.0 copy-start
  11.0 0.2 fusion.56
  11.2 1.0 collective-permute-start.1
  12.2 0.0 collective-permute-start
  12.2 9.5 %collective-permute-done.1 = f32[4,192,16]{2,1,0:T(8,128)S(1)} collective-permute-done((f32[4,192,16]{2,1,0:T(8,128)S(1)}, f32[4,192,16]{2,1,0:T(8,128)S(1)}, u32[]{:S(2)}, u32[]{:S(2)}) %collective-permute-start.1) | collective-permute-done | bytes 49184 | tf_op jit(solution)/shard_map/ppermute | solution.py:29
  21.7 0.0 copy-done
  21.7 0.0 copy-start.1
  21.7 0.7 copy-done.1
  22.4 0.4 collective-permute-done
  22.8 3.8 %concatenate.15 = f32[4,192,1056]{2,1,0:T(8,128)S(1)} concatenate(f32[4,192,16]{2,1,0:T(8,128)} %collective-permute-done, f32[4,192,1024]{2,1,0:T(8,128)} %bitcast.51, f32[4,192,16]{2,1,0:T(8,128)} %copy-done.1), dimensions={2} | concatenate | bytes 6488064 | tf_op jit(solution)/shard_map/concatenate | solution.py:130
  26.7 2.7 fusion.55
  29.3 3.4 %collective-permute-start.2 = (f32[3,192,1056]{2,1,0:T(8,128)}, f32[3,192,1056]{2,1,0:T(8,128)}, u32[]{:S(2)}, u32[]{:S(2)}) collective-permute-start(f32[3,192,1056]{2,1,0:T(8,128)} %get-tuple-element.8), channel_id=1, source_target_pairs={{0,4},{4,8},{8,12},{12,16},{16,20},{20,24},{24,28},{1,5},{5,9},{9,... | collective-permute-start | bytes 7299080 | tf_op jit(solution)/shard_map/ppermute | solution.py:26
  32.8 3.3 %collective-permute-start.3 = (f32[3,192,1056]{2,1,0:T(8,128)}, f32[3,192,1056]{2,1,0:T(8,128)}, u32[]{:S(2)}, u32[]{:S(2)}) collective-permute-start(f32[3,192,1056]{2,1,0:T(8,128)} %get-tuple-element.9), channel_id=1, source_target_pairs={{4,0},{8,4},{12,8},{16,12},{20,16},{24,20},{28,24},{5,1},{9,5},{13... | collective-permute-start | bytes 7299080 | tf_op jit(solution)/shard_map/ppermute | solution.py:29
  36.1 1.8 copy.45
  37.9 0.1 pad.17.clone
  38.0 0.7 fusion.57
  38.7 0.1 fusion.22
  38.8 1.8 maximum_maximum_fusion.info_ref
  40.6 51.4 %collective-permute-done.2 = f32[3,192,1056]{2,1,0:T(8,128)} collective-permute-done((f32[3,192,1056]{2,1,0:T(8,128)}, f32[3,192,1056]{2,1,0:T(8,128)}, u32[]{:S(2)}, u32[]{:S(2)}) %collective-permute-start.2) | collective-permute-done | bytes 2433056 | tf_op jit(solution)/shard_map/ppermute | solution.py:26
  92.0 56.8 %collective-permute-done.3 = f32[3,192,1056]{2,1,0:T(8,128)} collective-permute-done((f32[3,192,1056]{2,1,0:T(8,128)}, f32[3,192,1056]{2,1,0:T(8,128)}, u32[]{:S(2)}, u32[]{:S(2)}) %collective-permute-start.3) | collective-permute-done | bytes 2433056 | tf_op jit(solution)/shard_map/ppermute | solution.py:29
  148.8 5.8 %fusion = (bf16[10,192,1152]{2,1,0:T(8,128)(2,1)}, bf16[10,192,1152]{2,1,0:T(8,128)(2,1)}) fusion(f32[3,192,1056]{2,1,0:T(8,128)} %collective-permute-done.3, f32[4,192,1056]{2,1,0:T(8,128)S(1)} %concatenate.15, f32[3,192,1056]{2,1,0:T(8,128)} %collective-permute-done.2), kind=kLoop, calls=%fused_computation.2 | loop fusion | flops 22118400 | bytes 16957440 | tf_op jit(solution)/shard_map/convert_element_type | solution.py:137
  154.6 31.0 %shard_map.59 = f32[4,192,1024]{2,1,0:T(8,128)} custom-call(bf16[10,192,1152]{2,1,0:T(8,128)(2,1)} %get-tuple-element.3.hi_ref, bf16[10,192,1152]{2,1,0:T(8,128)(2,1)} %get-tuple-element.2.lo_ref, f32[4,24,1024]{2,1,0:T(8,128)} %maximum_maximum_fusion.info_ref), custom_call_target="tpu_custom_call" | custom-call | tf_op jit(solution)/shard_map/pallas_call | solution.py:106
  185.6 5.6 %copy.21 = f32[4,192,1024]{2,0,1:T(4,128)} copy(f32[4,192,1024]{2,1,0:T(8,128)} %shard_map.59) | data formatting | bytes 6291456 | tf_op jit(solution)/shard_map/pallas_call | solution.py:106
  191.1 3.9 %all-to-all-start = ((f32[4,192,1024]{2,0,1:T(4,128)}), f32[4,192,1024]{2,0,1:T(4,128)S(1)}, u32[]{:S(2)}, u32[]{:S(2)}) async-start(f32[4,192,1024]{2,0,1:T(4,128)} %copy.21), calls=%async_computation | async-start | bytes 6291456 | tf_op jit(solution)/shard_map/all_to_all | solution.py:156
  195.0 0.1 fusion.29
  195.2 0.1 sine_negate_fusion
  195.3 36.8 %all-to-all-done = f32[4,192,1024]{2,0,1:T(4,128)S(1)} async-done(((f32[4,192,1024]{2,0,1:T(4,128)}), f32[4,192,1024]{2,0,1:T(4,128)S(1)}, u32[]{:S(2)}, u32[]{:S(2)}) %all-to-all-start) | async-done | bytes 3145760 | tf_op jit(solution)/shard_map/all_to_all | solution.py:156
  232.1 3.7 %copy.44 = f32[4,4,48,1024]{3,1,2,0:T(4,128)} copy(f32[4,4,48,1024]{3,0,2,1:T(4,128)S(1)} %bitcast.52) | data formatting | bytes 6291456 | tf_op jit(solution)/shard_map/all_to_all | solution.py:156
  235.8 3.9 %all_to_all.16 = f32[4,48,4096]{2,1,0:T(8,128)S(1)} reshape(f32[4,48,4,1024]{3,2,1,0:T(4,128)} %bitcast.53) | data formatting | bytes 6291456 | tf_op jit(solution)/shard_map/all_to_all | solution.py:156
  239.7 3.7 %copy.23 = f32[48,4,4096]{2,1,0:T(4,128)} copy(f32[48,4,4096]{2,0,1:T(8,128)S(1)} %bitcast.54) | data formatting | bytes 6291456 | tf_op jit(solution)/shard_map/transpose | solution.py:157
  243.4 6.4 %reshape.169 = f32[192,64,64]{2,1,0:T(8,128)} reshape(f32[48,4,4096]{2,1,0:T(4,128)} %copy.23) | data formatting | bytes 6291456 | tf_op jit(solution)/shard_map/reshape | solution.py:36
  249.8 12.4 %fusion.12 = f32[192,64,128]{2,1,0:T(8,128)S(1)} fusion(f32[192,64,64]{2,1,0:T(8,128)} %reshape.169, f32[64,64]{1,0:T(8,128)S(1)} %get-tuple-element.21, f32[64,64]{1,0:T(8,128)S(1)} %get-tuple-element.22), kind=kOutput, calls=%fused_computation.36 | convolution fusion | flops 1207967744 | bytes 9469952 | tf_op jit(solution)/shard_map/rab,ac->rbc/dot_general | solution.py:42
  262.2 3.2 %multiply_add_fusion = (f32[192,64,64]{2,1,0:T(8,128)S(1)}, f32[192,64,64]{2,1,0:T(8,128)S(1)}) fusion(f32[192,64,128]{2,1,0:T(8,128)S(1)} %fusion.12, f32[64,64]{1,0:T(8,128)S(1)} %get-tuple-element.23, f32[64,64]{1,0:T(8,128)S(1)} %get-tuple-element.24), kind=kLoop, calls=%fused_computation.8 | loop fusion | flops 4718592 | bytes 12615680 | tf_op jit(solution)/shard_map/add | solution.py:54
  265.5 4.2 %fusion.7 = f32[192,20,128]{2,1,0:T(8,128)S(1)} fusion(f32[192,64,64]{2,1,0:T(8,128)S(1)} %get-tuple-element.5, f32[192,64,64]{2,1,0:T(8,128)S(1)} %get-tuple-element.4), kind=kOutput, calls=%fused_computation.20 | convolution fusion | flops 379078144 | bytes 8257536 | tf_op jit(solution)/shard_map/rbc,bq->rqc/dot_general | solution.py:61
  269.7 4.4 %fusion.6 = f32[192,20,128]{2,1,0:T(8,128)S(1)} fusion(f32[192,64,64]{2,1,0:T(8,128)S(1)} %get-tuple-element.5, f32[192,64,64]{2,1,0:T(8,128)S(1)} %get-tuple-element.4), kind=kOutput, calls=%fused_computation.19 | convolution fusion | flops 379078144 | bytes 8257536 | tf_op jit(solution)/shard_map/rbc,bq->rqc/dot_general | solution.py:60
  274.1 2.7 fusion.2
  276.8 2.9 %reshape.171 = f32[48,4,1280]{2,1,0:T(4,128)} reshape(f32[192,20,64]{2,1,0:T(8,128)} %get-tuple-element.6) | data formatting | bytes 1966080 | tf_op jit(solution)/shard_map/reshape | solution.py:65
  279.7 1.6 reshape.170
  (3 shorter events, 0.0 us)
Async XLA Ops:
  11.0 10.6 %copy-start = (f32[4,6,32,1024]{3,2,1,0:T(8,128)}, f32[4,6,32,1024]{3,2,1,0:T(8,128)S(1)}, u32[]{:S(2)}) copy-start(f32[4,6,32,1024]{3,2,1,0:T(8,128)S(1)} %copy.17) | copy-start | bytes 9437188
  11.2 10.4 %collective-permute-start.1 = (f32[4,192,16]{2,1,0:T(8,128)S(1)}, f32[4,192,16]{2,1,0:T(8,128)S(1)}, u32[]{:S(2)}, u32[]{:S(2)}) collective-permute-start(f32[4,192,16]{2,1,0:T(8,128)S(1)} %get-tuple-element.10), channel_id=1, source_target_pairs={{1,0},{2,1},{3,2},{0,3},{5,4},{6,5},{7,6},{4,7},{9,8},{10,9},{11,1... | collective-permute-start | bytes 147464 | tf_op jit(solution)/shard_map/ppermute | solution.py:29
  12.2 10.6 %collective-permute-start = (f32[4,192,16]{2,1,0:T(8,128)S(1)}, f32[4,192,16]{2,1,0:T(8,128)}, u32[]{:S(2)}, u32[]{:S(2)}) collective-permute-start(f32[4,192,16]{2,1,0:T(8,128)S(1)} %get-tuple-element.11), channel_id=1, source_target_pairs={{0,1},{1,2},{2,3},{3,0},{4,5},{5,6},{6,7},{7,4},{8,9},{9,10},{10,1... | collective-permute-start | bytes 147464 | tf_op jit(solution)/shard_map/ppermute | solution.py:26
  21.7 0.7 copy-start.1
  29.3 62.7 %collective-permute-start.2 = (f32[3,192,1056]{2,1,0:T(8,128)}, f32[3,192,1056]{2,1,0:T(8,128)}, u32[]{:S(2)}, u32[]{:S(2)}) collective-permute-start(f32[3,192,1056]{2,1,0:T(8,128)} %get-tuple-element.8), channel_id=1, source_target_pairs={{0,4},{4,8},{8,12},{12,16},{16,20},{20,24},{24,28},{1,5},{5,9},{9,... | collective-permute-start | bytes 7299080 | tf_op jit(solution)/shard_map/ppermute | solution.py:26
  32.8 116.0 %collective-permute-start.3 = (f32[3,192,1056]{2,1,0:T(8,128)}, f32[3,192,1056]{2,1,0:T(8,128)}, u32[]{:S(2)}, u32[]{:S(2)}) collective-permute-start(f32[3,192,1056]{2,1,0:T(8,128)} %get-tuple-element.9), channel_id=1, source_target_pairs={{4,0},{8,4},{12,8},{16,12},{20,16},{24,20},{28,24},{5,1},{9,5},{13... | collective-permute-start | bytes 7299080 | tf_op jit(solution)/shard_map/ppermute | solution.py:29
  191.1 41.0 %all-to-all-start = ((f32[4,192,1024]{2,0,1:T(4,128)}), f32[4,192,1024]{2,0,1:T(4,128)S(1)}, u32[]{:S(2)}, u32[]{:S(2)}) async-start(f32[4,192,1024]{2,0,1:T(4,128)} %copy.21), calls=%async_computation | async-start | bytes 6291456 | tf_op jit(solution)/shard_map/all_to_all | solution.py:156

commit v2 on v1

--- a/solution.py
+++ b/solution.py
@@ -65,10 +65,14 @@
     return (real_part.reshape(n_items, n_lines, NK), imag_part.reshape(n_items, n_lines, NK))
 
 
-def interp_kernel(hi_ref, lo_ref, info_ref, out_ref):
-    row = pl.program_id(0)
-    block = pl.program_id(1)
-    info = info_ref[0]
+def interp_kernel(*refs):
+    span = 2 * ROWS_OUT + 1
+    hi_refs = refs[:span]
+    lo_refs = refs[span : 2 * span]
+    info_ref = refs[2 * span]
+    out_ref = refs[2 * span + 1]
+    block = pl.program_id(0)
+    info = info_ref[...]
     offset_r = info[16:17, :]
     offset_d = info[17:18, :]
     c_index = lax.broadcasted_iota(jnp.int32, (WINDOW, LANES), 0).astype(jnp.float32)
@@ -76,8 +80,8 @@
     tap = c_index - j_index - offset_d
     masks = [tap == float(b) for b in range(TAPS)]
     start = pl.multiple_of(block * LANES, LANES)
-    acc = jnp.zeros(out_ref.shape[1:], jnp.float32)
-    for p in range(2 * ROWS_OUT + 1):
+    acc = jnp.zeros(out_ref.shape, jnp.float32)
+    for p in range(span):
         picked = []
         for b in range(TAPS):
             value = jnp.zeros_like(offset_r)
@@ -92,29 +96,38 @@
         )
         m_hi = matrix.astype(jnp.bfloat16)
         m_lo = (matrix - m_hi.astype(jnp.float32)).astype(jnp.bfloat16)
-        x_hi = hi_ref[row + p, :, pl.ds(start, WINDOW)]
-        x_lo = lo_ref[row + p, :, pl.ds(start, WINDOW)]
+        x_hi = hi_refs[p][:, pl.ds(start, WINDOW)]
+        x_lo = lo_refs[p][:, pl.ds(start, WINDOW)]
         acc = acc + jnp.dot(x_hi, m_hi, preferred_element_type=jnp.float32)
         acc = acc + jnp.dot(x_hi, m_lo, preferred_element_type=jnp.float32)
         acc = acc + jnp.dot(x_lo, m_hi, preferred_element_type=jnp.float32)
-    out_ref[0] = acc
-
-
-def interpolate(x_hi, x_lo, info, lat_rows, lon_cols):
-    n_rows, n_items, width = x_hi.shape
+    out_ref[...] = acc
+
+
+def interpolate_row(his, los, info_row, lon_cols):
+    n_items, width = his[0].shape
     blocks = lon_cols // LANES
+    whole = pl.BlockSpec((n_items, width), lambda jb: (0, 0))
     return pl.pallas_call(
         interp_kernel,
-        out_shape=jax.ShapeDtypeStruct((lat_rows, n_items, lon_cols), jnp.float32),
-        grid=(lat_rows, blocks),
-        in_specs=[
-            pl.BlockSpec((n_rows, n_items, width), lambda i, jb: (0, 0, 0)),
-            pl.BlockSpec((n_rows, n_items, width), lambda i, jb: (0, 0, 0)),
-            pl.BlockSpec((1, info.shape[1], LANES), lambda i, jb: (i, 0, jb)),
-        ],
-        out_specs=pl.BlockSpec((1, n_items, LANES), lambda i, jb: (i, 0, jb)),
-        compiler_params=pltpu.CompilerParams(vmem_limit_bytes=60 * 1024 * 1024),
-    )(x_hi, x_lo, info)
+        out_shape=jax.ShapeDtypeStruct((n_items, lon_cols), jnp.float32),
+        grid=(blocks,),
+        in_specs=[whole] * (2 * len(his)) + [pl.BlockSpec((info_row.shape[0], LANES), lambda jb: (0, jb))],
+        out_specs=pl.BlockSpec((n_items, LANES), lambda jb: (0, jb)),
+        compiler_params=pltpu.CompilerParams(vmem_limit_bytes=48 * 1024 * 1024),
+    )(*his, *los, info_row)
+
+
+def split_row(row, width):
+    padded = jnp.pad(row, ((0, 0), (0, width - row.shape[1])))
+    rounded = lax.reduce_precision(padded, exponent_bits=8, mantissa_bits=7)
+    return rounded.astype(jnp.bfloat16), (padded - rounded).astype(jnp.bfloat16)
+
+
+def ready_step(i, lat_rows):
+    below = ROWS_OUT - 1 - i if i < ROWS_OUT else -1
+    above = i + ROWS_OUT - lat_rows
+    return max(below, above)
 
 
 def on_device(fields, weights, stencil, bands):
@@ -128,13 +141,25 @@
     tile = mixed.reshape(lat_rows, n_items, lon_cols)
     left, right = shifted(tile, "lon", HALO, 2, True)
     wide = jnp.concatenate([left, tile, right], axis=2)
-    below, above = shifted(wide, "lat", ROWS_OUT, 0, False)
-    haloed = jnp.concatenate([below, wide, above], axis=0)
+
+    count = lax.axis_size("lat")
+    forward = [(i, i + 1) for i in range(count - 1)]
+    backward = [(target, source) for source, target in forward]
+    below = [None] * ROWS_OUT
+    above = [None] * ROWS_OUT
+    previous = None
+    for step in range(ROWS_OUT):
+        h_below = ROWS_OUT - 1 - step
+        src_below = wide[lat_rows - ROWS_OUT + h_below]
+        src_above = wide[step]
+        if previous is not None:
+            src_below, src_above, _ = lax.optimization_barrier((src_below, src_above, previous))
+        below[h_below] = lax.ppermute(src_below, "lat", forward)
+        above[step] = lax.ppermute(src_above, "lat", backward)
+        previous = (below[h_below], above[step])
+    rows = below + [wide[i] for i in range(lat_rows)] + above
     width = lon_cols + LANES
-    haloed = jnp.pad(haloed, ((0, 0), (0, 0), (0, width - haloed.shape[2])))
-    rounded = lax.reduce_precision(haloed, exponent_bits=8, mantissa_bits=7)
-    x_hi = rounded.astype(jnp.bfloat16)
-    x_lo = (haloed - rounded).astype(jnp.bfloat16)
+    split = [split_row(r, width) for r in rows]
 
     lat_start = lax.axis_index("lat") * lat_rows
     lon_start = lax.axis_index("lon") * lon_cols
@@ -152,11 +177,18 @@
         ],
         axis=1,
     )
-    departed = interpolate(x_hi, x_lo, info, lat_rows, lon_cols)
-    gathered = lax.all_to_all(departed, "lon", split_axis=1, concat_axis=2, tiled=True)
-    lines = jnp.transpose(gathered, (1, 0, 2))
-    real_part, imag_part = spectrum(lines)
-    return (real_part, imag_part)
+    span = 2 * ROWS_OUT + 1
+    real_rows = [None] * lat_rows
+    imag_rows = [None] * lat_rows
+    for i in sorted(range(lat_rows), key=lambda i: ready_step(i, lat_rows)):
+        his = [split[i + p][0] for p in range(span)]
+        los = [split[i + p][1] for p in range(span)]
+        departed = interpolate_row(his, los, info[i], lon_cols)
+        gathered = lax.all_to_all(departed, "lon", split_axis=0, concat_axis=1, tiled=True)
+        real_part, imag_part = spectrum(gathered[:, None, :])
+        real_rows[i] = real_part
+        imag_rows[i] = imag_part
+    return (jnp.concatenate(real_rows, axis=1), jnp.concatenate(imag_rows, axis=1))
 
 
 def solution(mesh):

time: 282 us -> 287 us (1.018)
  waiting for transfers between devices: 155 us -> 101 us
  starting transfers between devices: 11.6 us -> 37.8 us
  local copies, waits for them, and re-layouts: 40.4 us -> 62.2 us
  matrix products: 21 us -> 24.9 us
    ppermute x0 -> x6, waiting for transfers between devices: none -> 89.9 us  [the longest x3 75.6 us: on_device(): above[step] = lax.ppermute(src_above, 'lat', backward)]
    ppermute x2 -> x1, waiting for transfers between devices: 66.2 us -> 7.3 us  [shifted(): lax.ppermute(lax.slice_in_dim(block, 0, width, axis=dim), axis, backward)]
    ppermute x2 -> x1, waiting for transfers between devices: 51.8 us -> 1.03 us  [shifted(): lax.ppermute(lax.slice_in_dim(block, block.shape[dim] - width, None, axis...]
    all_to_all x1 -> x4, waiting for transfers between devices: 36.8 us -> 3.03 us  [on_device(): lax.all_to_all(departed, 'lon', split_axis=0, concat_axis=1, tiled=True)]
    another operation x0 -> x4, local copies, waits for them, and re-layouts: none -> 23.3 us  [spectrum(): folded = block.reshape(n_items * n_lines, RADIX, RADIX)]
    ppermute x0 -> x6, starting transfers between devices: none -> 19.6 us  [the longest x3 11.9 us: on_device(): below[h_below] = lax.ppermute(src_below, 'lat', forward)]
    all_to_all x1 -> x4, starting transfers between devices: 3.88 us -> 17.2 us  [on_device(): lax.all_to_all(departed, 'lon', split_axis=0, concat_axis=1, tiled=True)]
    reshape x1 -> x0, local copies, waits for them, and re-layouts: 6.37 us -> none  [spectrum(): folded = block.reshape(n_items * n_lines, RADIX, RADIX)]
  transfers between devices with their start and end apart: 5 -> 12, of which waited for: 5 -> 7; matrix products, arithmetic and copies ran while one was open for 2% -> 11% of each run, Pallas kernels for 0% -> 12%
where the time goes in v2:
time: 287 us; the launch traced here: 285 us
  waiting for transfers between devices  101 us (35%)
  local copies, waits for them, and re-layouts  62.2 us (22%)
  starting transfers between devices  37.8 us (13%)
  Pallas kernels  33.6 us (12%)
  matrix products  24.9 us (9%)
  other arithmetic  23.7 us (8%)
    ppermute x3, waiting for transfers between devices, on_device(): above[step] = lax.ppermute(src_above, 'lat', backward)  75.6 us
    pallas_call x4, Pallas kernels, interpolate_row(): pl.pallas_call(interp_kernel, out_shape=jax.ShapeDtypeStruct((n_items, lo...  33.6 us
    another operation x4, local copies, waits for them, and re-layouts, spectrum(): folded = block.reshape(n_items * n_lines, RADIX, RADIX)  23.3 us
    all_to_all x4, starting transfers between devices, on_device(): lax.all_to_all(departed, 'lon', split_axis=0, concat_axis=1, tiled=True)  17.2 us
    dot_general x4, matrix products, spectrum(): jnp.einsum('rab,ac->rbc', folded, first_table, precision=highest)  15.5 us
    ppermute x3, waiting for transfers between devices, on_device(): below[h_below] = lax.ppermute(src_below, 'lat', forward)  14.3 us
    ppermute x3, starting transfers between devices, on_device(): below[h_below] = lax.ppermute(src_below, 'lat', forward)  11.9 us
    all_to_all x4, local copies, waits for them, and re-layouts, on_device(): lax.all_to_all(departed, 'lon', split_axis=0, concat_axis=1, tiled=True)  10.1 us
  transfers between devices with their start and end apart: 12, of which 7 were waited for; matrix products, arithmetic and copies ran while one was open for 11% of the time, Pallas kernels for 12%

profile of v2, /device:TPU:24, one launch (start us, length us, event | category | flops | bytes accessed | tf_op | source)
XLA Modules:
  0.0 285.0 jit_solution(7044793795331584210)
XLA Ops:
  1.4 7.3 %multiply_add_fusion = f32[4,6,32,1024]{3,0,2,1:T(4,128)S(1)} fusion(f32[4,6,32,1024]{3,0,2,1:T(4,128)} %bitcast.105, f32[6,32]{1,0:T(8,128)S(1)} %get-tuple-element.71, f32[6,32]{1,0:T(8,128)S(1)} %get-tuple-element.72, f32[6,32]{1,0:T(8,128)S(1)} %get-tuple-element.69, f32[6,32]{1,0:T(8,128)S(1)} %get-tuple-element.70, f32[6,32]{1,0:T(8,128)S(1)} %get-tuple-element.68), kind=kLoop, calls=%fused_computation | loop fusion | flops 7077888 | bytes 6295296 | tf_op jit(solution)/shard_map/add | solution.py:140
  8.7 1.8 copy.32
  14.9 7.3 %collective-permute-done.1 = f32[4,192,16]{2,1,0:T(8,128)S(1)} collective-permute-done((f32[4,192,16]{2,1,0:T(8,128)}, f32[4,192,16]{2,1,0:T(8,128)S(1)}, u32[]{:S(2)}, u32[]{:S(2)}) %collective-permute-start.1) | collective-permute-done | bytes 49184 | tf_op jit(solution)/shard_map/ppermute | solution.py:29
  23.3 4.3 %concatenate.30 = f32[4,192,1056]{2,1,0:T(8,128)} concatenate(f32[4,192,16]{2,1,0:T(8,128)} %collective-permute-done, f32[4,192,1024]{2,1,0:T(8,128)S(1)} %bitcast.100, f32[4,192,16]{2,1,0:T(8,128)S(1)} %collective-permute-done.1), dimensions={2} | concatenate | bytes 6488064 | tf_op jit(solution)/shard_map/concatenate | solution.py:143
  27.6 3.2 %slice_bitcast_fusion.1 = (f32[192,1056]{1,0:T(8,128)S(1)}, f32[192,1056]{1,0:T(8,128)S(1)}, f32[192,1056]{1,0:T(8,128)}, f32[192,1056]{1,0:T(8,128)S(1)}) fusion(f32[4,192,1056]{2,1,0:T(8,128)} %concatenate.30), kind=kLoop, calls=%fused_computation.56 | loop fusion | bytes 6488064 | tf_op jit(solution)/shard_map/squeeze | solution.py:153
  30.7 3.4 %collective-permute-start.2 = (f32[192,1056]{1,0:T(8,128)S(1)}, f32[192,1056]{1,0:T(8,128)S(1)}, u32[]{:S(2)}, u32[]{:S(2)}) collective-permute-start(f32[192,1056]{1,0:T(8,128)S(1)} %get-tuple-element.14), channel_id=1, source_target_pairs={{0,4},{4,8},{8,12},{12,16},{16,20},{20,24},{24,28},{1,5},{5,9},{9,... | collective-permute-start | bytes 2433032 | tf_op jit(solution)/shard_map/ppermute | solution.py:157
  34.2 3.3 %collective-permute-start.3 = (f32[192,1056]{1,0:T(8,128)S(1)}, f32[192,1056]{1,0:T(8,128)S(1)}, u32[]{:S(2)}, u32[]{:S(2)}) collective-permute-start(f32[192,1056]{1,0:T(8,128)S(1)} %get-tuple-element.15), channel_id=1, source_target_pairs={{4,0},{8,4},{12,8},{16,12},{20,16},{24,20},{28,24},{5,1},{9,5},{13... | collective-permute-start | bytes 2433032 | tf_op jit(solution)/shard_map/ppermute | solution.py:158
  38.7 1.4 fusion.6
  40.1 14.3 %collective-permute-done.2 = f32[192,1056]{1,0:T(8,128)S(1)} collective-permute-done((f32[192,1056]{1,0:T(8,128)S(1)}, f32[192,1056]{1,0:T(8,128)S(1)}, u32[]{:S(2)}, u32[]{:S(2)}) %collective-permute-start.2) | collective-permute-done | bytes 811040 | tf_op jit(solution)/shard_map/ppermute | solution.py:157
  54.4 18.9 %collective-permute-done.3 = f32[192,1056]{1,0:T(8,128)S(1)} collective-permute-done((f32[192,1056]{1,0:T(8,128)S(1)}, f32[192,1056]{1,0:T(8,128)S(1)}, u32[]{:S(2)}, u32[]{:S(2)}) %collective-permute-start.3) | collective-permute-done | bytes 811040 | tf_op jit(solution)/shard_map/ppermute | solution.py:158
  73.3 2.4 collective-permute-start.5
  75.9 3.5 %collective-permute-start.4 = (f32[192,1056]{1,0:T(8,128)}, f32[192,1056]{1,0:T(8,128)}, u32[]{:S(2)}, u32[]{:S(2)}) collective-permute-start(f32[192,1056]{1,0:T(8,128)} %get-tuple-element.9), channel_id=1, source_target_pairs={{0,4},{4,8},{8,12},{12,16},{16,20},{20,24},{24,28},{1,5},{5,9},{9,... | collective-permute-start | bytes 2433032 | tf_op jit(solution)/shard_map/ppermute | solution.py:157
  79.7 36.0 %collective-permute-done.5 = f32[192,1056]{1,0:T(8,128)S(1)} collective-permute-done((f32[192,1056]{1,0:T(8,128)S(1)}, f32[192,1056]{1,0:T(8,128)S(1)}, u32[]{:S(2)}, u32[]{:S(2)}) %collective-permute-start.5) | collective-permute-done | bytes 811040 | tf_op jit(solution)/shard_map/ppermute | solution.py:158
  116.6 8.5 %shard_map.61 = f32[192,1024]{1,0:T(8,128)} custom-call(bf16[192,1152]{1,0:T(8,128)(2,1)S(1)} %get-tuple-element.41.refs_2_.refs_1_.refs_0_, bf16[192,1152]{1,0:T(8,128)(2,1)S(1)} %get-tuple-element.55.refs_3_.refs_2_.refs_1_.refs_0_, bf16[192,1152]{1,0:T(8,128)(2,1)S(1)} %get-tuple-element.73.refs_4_.refs_3_.refs_2_.refs_1_, ...), custom_call_target="tpu_custom_call" | custom-call | tf_op jit(solution)/shard_map/pallas_call | solution.py:111
  125.1 4.2 %all-to-all-start.2 = ((f32[4,48,1024]{2,1,0:T(8,128)}), f32[4,48,1024]{2,1,0:T(8,128)}, u32[]{:S(2)}, u32[]{:S(2)}) async-start(f32[4,48,1024]{2,1,0:T(8,128)} %bitcast.104), calls=%async_computation.2 | async-start | bytes 1572864 | tf_op jit(solution)/shard_map/all_to_all | solution.py:187
  129.4 2.1 collective-permute-start.7
  132.8 8.4 %shard_map.60 = f32[192,1024]{1,0:T(8,128)} custom-call(bf16[192,1152]{1,0:T(8,128)(2,1)S(1)} %get-tuple-element.39.refs_1_.refs_0_, bf16[192,1152]{1,0:T(8,128)(2,1)S(1)} %copy-done.5, bf16[192,1152]{1,0:T(8,128)(2,1)S(1)} %get-tuple-element.55.refs_3_.refs_2_.refs_1_.refs_0_, bf16[192,1152]{1,0:T(8,128)(2,1)S(1)} %get-tuple-element.73.refs_4_.refs_3_.refs_2_.refs_1_, ...), custom_call_target="tpu_custom_call" | custom-call | tf_op jit(solution)/shard_map/pallas_call | solution.py:111
  142.7 4.2 %all-to-all-start.1 = ((f32[4,48,1024]{2,1,0:T(8,128)}), f32[4,48,1024]{2,1,0:T(8,128)}, u32[]{:S(2)}, u32[]{:S(2)}) async-start(f32[4,48,1024]{2,1,0:T(8,128)} %bitcast.102), calls=%async_computation.1 | async-start | bytes 1572864 | tf_op jit(solution)/shard_map/all_to_all | solution.py:187
  147.0 5.0 %collective-permute-start.6 = (f32[192,1056]{1,0:T(8,128)}, f32[192,1056]{1,0:T(8,128)}, u32[]{:S(2)}, u32[]{:S(2)}) collective-permute-start(f32[192,1056]{1,0:T(8,128)} %copy-done.25), channel_id=1, source_target_pairs={{0,4},{4,8},{8,12},{12,16},{16,20},{20,24},{24,28},{1,5},{5,9},{9,... | collective-permute-start | bytes 2433032 | tf_op jit(solution)/shard_map/ppermute | solution.py:157
  151.9 20.7 %collective-permute-done.7 = f32[192,1056]{1,0:T(8,128)} collective-permute-done((f32[192,1056]{1,0:T(8,128)}, f32[192,1056]{1,0:T(8,128)}, u32[]{:S(2)}, u32[]{:S(2)}) %collective-permute-start.7) | collective-permute-done | bytes 811040 | tf_op jit(solution)/shard_map/ppermute | solution.py:158
  172.7 2.0 fusion.10
  175.6 8.4 %shard_map.62 = f32[192,1024]{1,0:T(8,128)} custom-call(bf16[192,1152]{1,0:T(8,128)(2,1)S(1)} %get-tuple-element.55.refs_3_.refs_2_.refs_1_.refs_0_, bf16[192,1152]{1,0:T(8,128)(2,1)S(1)} %get-tuple-element.73.refs_4_.refs_3_.refs_2_.refs_1_, bf16[192,1152]{1,0:T(8,128)(2,1)S(1)} %get-tuple-element.51.refs_5_.refs_4_.refs_3_.refs_2_, ...), custom_call_target="tpu_custom_call" | custom-call | tf_op jit(solution)/shard_map/pallas_call | solution.py:111
  184.0 4.4 %all-to-all-start.3 = ((f32[4,48,1024]{2,1,0:T(8,128)}), f32[4,48,1024]{2,1,0:T(8,128)}, u32[]{:S(2)}, u32[]{:S(2)}) async-start(f32[4,48,1024]{2,1,0:T(8,128)} %bitcast.101), calls=%async_computation.3 | async-start | bytes 1572864 | tf_op jit(solution)/shard_map/all_to_all | solution.py:187
  190.0 2.5 copy.40
  192.6 2.5 copy.38
  195.1 2.9 %reshape_broadcast_in_dim.13 = f32[48,64,64]{2,1,0:T(8,128)} reshape(f32[48,4,1024]{2,1,0:T(4,128)} %copy.38) | data formatting | bytes 1572864 | tf_op jit(solution)/shard_map/reshape;broadcast_in_dim | solution.py:36
  198.0 2.9 %reshape_broadcast_in_dim.14 = f32[48,64,64]{2,1,0:T(8,128)} reshape(f32[48,4,1024]{2,1,0:T(4,128)} %copy.40) | data formatting | bytes 1572864 | tf_op jit(solution)/shard_map/reshape;broadcast_in_dim | solution.py:36
  200.8 1.4 fusion.1
  202.4 8.3 %shard_map.59 = f32[192,1024]{1,0:T(8,128)} custom-call(bf16[192,1152]{1,0:T(8,128)(2,1)S(1)} %get-tuple-element.37.refs_0_, bf16[192,1152]{1,0:T(8,128)(2,1)S(1)} %copy-done.15, bf16[192,1152]{1,0:T(8,128)(2,1)S(1)} %copy-done.6, bf16[192,1152]{1,0:T(8,128)(2,1)S(1)} %get-tuple-element.55.refs_3_.refs_2_.refs_1_.refs_0_, ...), custom_call_target="tpu_custom_call" | custom-call | tf_op jit(solution)/shard_map/pallas_call | solution.py:111
  210.7 4.3 %all-to-all-start = ((f32[4,48,1024]{2,1,0:T(8,128)}), f32[4,48,1024]{2,1,0:T(8,128)}, u32[]{:S(2)}, u32[]{:S(2)}) async-start(f32[4,48,1024]{2,1,0:T(8,128)} %bitcast.103), calls=%async_computation | async-start | bytes 1572864 | tf_op jit(solution)/shard_map/all_to_all | solution.py:187
  215.1 3.5 %fusion.107 = f32[48,64,128]{2,1,0:T(8,128)S(1)} fusion(f32[48,64,64]{2,1,0:T(8,128)S(1)} %copy-done.23, f32[64,128,1]{1,0,2:T(8,128)} %maximum_bitcast_fusion), kind=kOutput, calls=%fused_computation.184 | convolution fusion | flops 301989888 | bytes 2392064 | tf_op jit(solution)/shard_map/rab,ac->rbc/dot_general | solution.py:42
  218.6 2.6 fusion.108
  221.2 2.5 copy.42
  223.7 3.0 %all-to-all-done = f32[4,48,1024]{2,1,0:T(8,128)} async-done(((f32[4,48,1024]{2,1,0:T(8,128)}), f32[4,48,1024]{2,1,0:T(8,128)}, u32[]{:S(2)}, u32[]{:S(2)}) %all-to-all-start) | async-done | bytes 786464 | tf_op jit(solution)/shard_map/all_to_all | solution.py:187
  226.8 2.5 copy.36
  229.3 2.8 reshape_broadcast_in_dim.12
  232.1 5.2 %fusion.106 = f32[48,64,128]{2,1,0:T(8,128)} fusion(f32[48,64,64]{2,1,0:T(8,128)} %reshape_broadcast_in_dim.12, f32[64,128,1]{1,0,2:T(8,128)S(1)} %copy-done.31), kind=kOutput, calls=%fused_computation.183 | convolution fusion | flops 301989888 | bytes 2392064 | tf_op jit(solution)/shard_map/rab,ac->rbc/dot_general | solution.py:42
  237.3 14.8 %reshape_broadcast_in_dim.15 = f32[48,64,64]{2,1,0:T(8,128)} reshape(f32[48,4,1024]{2,1,0:T(4,128)} %copy.42) | data formatting | bytes 1572864 | tf_op jit(solution)/shard_map/reshape;broadcast_in_dim | solution.py:36
  252.1 4.2 %fusion.109 = f32[48,64,128]{2,1,0:T(8,128)S(1)} fusion(f32[48,64,64]{2,1,0:T(8,128)} %reshape_broadcast_in_dim.15, f32[64,128,1]{1,0,2:T(8,128)S(1)} %copy-done.31), kind=kOutput, calls=%fused_computation.186 | convolution fusion | flops 301989888 | bytes 2392064 | tf_op jit(solution)/shard_map/rab,ac->rbc/dot_general | solution.py:42
  256.4 2.5 multiply_add_fusion.4
  268.3 1.4 fusion.14
  269.7 1.9 reshape.204
  271.6 1.9 reshape.200
  273.6 1.4 fusion.13
  274.9 1.9 reshape.205
  276.9 1.9 reshape.201
  281.4 1.6 copy.45
  283.3 1.6 copy.44
  (119 shorter events, 26.5 us)
Async XLA Ops:
  11.5 10.7 %collective-permute-start.1 = (f32[4,192,16]{2,1,0:T(8,128)}, f32[4,192,16]{2,1,0:T(8,128)S(1)}, u32[]{:S(2)}, u32[]{:S(2)}) collective-permute-start(f32[4,192,16]{2,1,0:T(8,128)} %get-tuple-element.18), channel_id=1, source_target_pairs={{1,0},{2,1},{3,2},{0,3},{5,4},{6,5},{7,6},{4,7},{9,8},{10,9},{11,1... | collective-permute-start | bytes 147464 | tf_op jit(solution)/shard_map/ppermute | solution.py:29
  12.4 10.8 %collective-permute-start = (f32[4,192,16]{2,1,0:T(8,128)}, f32[4,192,16]{2,1,0:T(8,128)}, u32[]{:S(2)}, u32[]{:S(2)}) collective-permute-start(f32[4,192,16]{2,1,0:T(8,128)} %get-tuple-element.19), channel_id=1, source_target_pairs={{0,1},{1,2},{2,3},{3,0},{4,5},{5,6},{6,7},{7,4},{8,9},{9,10},{10,1... | collective-permute-start | bytes 147464 | tf_op jit(solution)/shard_map/ppermute | solution.py:26
  27.6 9.9 %copy-start.35 = (s32[1,4,1024]{2,1,0:T(4,128)S(1)}, s32[1,4,1024]{2,1,0:T(4,128)}, u32[]{:S(2)}) copy-start(s32[1,4,1024]{2,1,0:T(4,128)} %get-tuple-element.67) | copy-start | bytes 49156
  27.6 9.9 %copy-start.36 = (s32[1024]{0:T(1024)S(1)}, s32[1024]{0:T(1024)}, u32[]{:S(2)}) copy-start(s32[1024]{0:T(1024)} %iota_add_fusion) | copy-start | bytes 12292
  27.6 9.9 %copy-start.37 = (s32[4]{0:T(128)S(1)}, s32[4]{0:T(128)}, u32[]{:S(2)}) copy-start(s32[4]{0:T(128)} %iota_add_fusion.1) | copy-start | bytes 52
  27.6 10.0 %copy-start.32 = (f32[16,4,1024]{2,1,0:T(4,128)S(1)}, f32[16,4,1024]{2,1,0:T(4,128)}, u32[]{:S(2)}) copy-start(f32[16,4,1024]{2,1,0:T(4,128)} %param.5) | copy-start | bytes 786436
  30.7 45.0 %copy-start.25 = (f32[192,1056]{1,0:T(8,128)}, f32[192,1056]{1,0:T(8,128)S(1)}, u32[]{:S(2)}) copy-start(f32[192,1056]{1,0:T(8,128)S(1)} %get-tuple-element.8) | copy-start | bytes 2433028
  30.7 23.7 %collective-permute-start.2 = (f32[192,1056]{1,0:T(8,128)S(1)}, f32[192,1056]{1,0:T(8,128)S(1)}, u32[]{:S(2)}, u32[]{:S(2)}) collective-permute-start(f32[192,1056]{1,0:T(8,128)S(1)} %get-tuple-element.14), channel_id=1, source_target_pairs={{0,4},{4,8},{8,12},{12,16},{16,20},{20,24},{24,28},{1,5},{5,9},{9,... | collective-permute-start | bytes 2433032 | tf_op jit(solution)/shard_map/ppermute | solution.py:157
  34.2 39.1 %collective-permute-start.3 = (f32[192,1056]{1,0:T(8,128)S(1)}, f32[192,1056]{1,0:T(8,128)S(1)}, u32[]{:S(2)}, u32[]{:S(2)}) collective-permute-start(f32[192,1056]{1,0:T(8,128)S(1)} %get-tuple-element.15), channel_id=1, source_target_pairs={{4,0},{8,4},{12,8},{16,12},{20,16},{24,20},{28,24},{5,1},{9,5},{13... | collective-permute-start | bytes 2433032 | tf_op jit(solution)/shard_map/ppermute | solution.py:158
  40.1 134.6 %copy-start = (bf16[192,1152]{1,0:T(8,128)(2,1)}, bf16[192,1152]{1,0:T(8,128)(2,1)S(1)}, u32[]{:S(2)}) copy-start(bf16[192,1152]{1,0:T(8,128)(2,1)S(1)} %get-tuple-element.76.refs_13_.refs_12_.refs_11_.refs_10_) | copy-start | bytes 1327108
  73.3 42.4 %collective-permute-start.5 = (f32[192,1056]{1,0:T(8,128)S(1)}, f32[192,1056]{1,0:T(8,128)S(1)}, u32[]{:S(2)}, u32[]{:S(2)}) collective-permute-start(f32[192,1056]{1,0:T(8,128)S(1)} %get-tuple-element.8), channel_id=1, source_target_pairs={{4,0},{8,4},{12,8},{16,12},{20,16},{24,20},{28,24},{5,1},{9,5},{13... | collective-permute-start | bytes 2433032 | tf_op jit(solution)/shard_map/ppermute | solution.py:158
  75.9 53.4 %collective-permute-start.4 = (f32[192,1056]{1,0:T(8,128)}, f32[192,1056]{1,0:T(8,128)}, u32[]{:S(2)}, u32[]{:S(2)}) collective-permute-start(f32[192,1056]{1,0:T(8,128)} %get-tuple-element.9), channel_id=1, source_target_pairs={{0,4},{4,8},{8,12},{12,16},{16,20},{20,24},{24,28},{1,5},{5,9},{9,... | collective-permute-start | bytes 2433032 | tf_op jit(solution)/shard_map/ppermute | solution.py:157
  79.5 37.0 %copy-start.1 = (bf16[192,1152]{1,0:T(8,128)(2,1)}, bf16[192,1152]{1,0:T(8,128)(2,1)S(1)}, u32[]{:S(2)}) copy-start(bf16[192,1152]{1,0:T(8,128)(2,1)S(1)} %get-tuple-element.40.refs_9_.refs_8_.refs_7_) | copy-start | bytes 1327108
  79.6 37.0 %copy-start.4 = (bf16[192,1152]{1,0:T(8,128)(2,1)}, bf16[192,1152]{1,0:T(8,128)(2,1)S(1)}, u32[]{:S(2)}) copy-start(bf16[192,1152]{1,0:T(8,128)(2,1)S(1)} %get-tuple-element.41.refs_2_.refs_1_.refs_0_) | copy-start | bytes 1327108
  79.7 45.4 %copy-start.7 = (bf16[192,1152]{1,0:T(8,128)(2,1)}, bf16[192,1152]{1,0:T(8,128)(2,1)S(1)}, u32[]{:S(2)}) copy-start(bf16[192,1152]{1,0:T(8,128)(2,1)S(1)} %get-tuple-element.46.refs_13_.refs_12_.refs_11_) | copy-start | bytes 1327108
  79.7 45.4 %copy-start.9 = (bf16[192,1152]{1,0:T(8,128)(2,1)}, bf16[192,1152]{1,0:T(8,128)(2,1)S(1)}, u32[]{:S(2)}) copy-start(bf16[192,1152]{1,0:T(8,128)(2,1)S(1)} %get-tuple-element.47.refs_6_.refs_5_.refs_4_) | copy-start | bytes 1327108
  116.6 8.5 %copy-start.17 = (bf16[192,1152]{1,0:T(8,128)(2,1)}, bf16[192,1152]{1,0:T(8,128)(2,1)S(1)}, u32[]{:S(2)}) copy-start(bf16[192,1152]{1,0:T(8,128)(2,1)S(1)} %get-tuple-element.45.refs_6_.refs_5_) | copy-start | bytes 1327108
  125.1 17.6 %all-to-all-start.2 = ((f32[4,48,1024]{2,1,0:T(8,128)}), f32[4,48,1024]{2,1,0:T(8,128)}, u32[]{:S(2)}, u32[]{:S(2)}) async-start(f32[4,48,1024]{2,1,0:T(8,128)} %bitcast.104), calls=%async_computation.2 | async-start | bytes 1572864 | tf_op jit(solution)/shard_map/all_to_all | solution.py:187
  129.3 3.4 %copy-start.2 = (bf16[192,1152]{1,0:T(8,128)(2,1)S(1)}, bf16[192,1152]{1,0:T(8,128)(2,1)}, u32[]{:S(2)}) copy-start(bf16[192,1152]{1,0:T(8,128)(2,1)} %copy-done.1) | copy-start | bytes 1327108
  129.3 3.4 %copy-start.5 = (bf16[192,1152]{1,0:T(8,128)(2,1)S(1)}, bf16[192,1152]{1,0:T(8,128)(2,1)}, u32[]{:S(2)}) copy-start(bf16[192,1152]{1,0:T(8,128)(2,1)} %copy-done.4) | copy-start | bytes 1327108
  129.4 3.4 %copy-start.10 = (bf16[192,1152]{1,0:T(8,128)(2,1)S(1)}, bf16[192,1152]{1,0:T(8,128)(2,1)}, u32[]{:S(2)}) copy-start(bf16[192,1152]{1,0:T(8,128)(2,1)} %copy-done.9) | copy-start | bytes 1327108
  129.4 3.4 %copy-start.21 = (f32[24,1024]{1,0:T(8,128)S(1)}, f32[24,1024]{1,0:T(8,128)}, u32[]{:S(2)}) copy-start(f32[24,1024]{1,0:T(8,128)} %get-tuple-element.59.refs_14_) | copy-start | bytes 294916
  129.4 43.3 %collective-permute-start.7 = (f32[192,1056]{1,0:T(8,128)}, f32[192,1056]{1,0:T(8,128)}, u32[]{:S(2)}, u32[]{:S(2)}) collective-permute-start(f32[192,1056]{1,0:T(8,128)} %get-tuple-element.9), channel_id=1, source_target_pairs={{4,0},{8,4},{12,8},{16,12},{20,16},{24,20},{28,24},{5,1},{9,5},{13... | collective-permute-start | bytes 2433032 | tf_op jit(solution)/shard_map/ppermute | solution.py:158
  142.7 41.3 %all-to-all-start.1 = ((f32[4,48,1024]{2,1,0:T(8,128)}), f32[4,48,1024]{2,1,0:T(8,128)}, u32[]{:S(2)}, u32[]{:S(2)}) async-start(f32[4,48,1024]{2,1,0:T(8,128)} %bitcast.102), calls=%async_computation.1 | async-start | bytes 1572864 | tf_op jit(solution)/shard_map/all_to_all | solution.py:187
  146.9 27.8 %copy-start.8 = (bf16[192,1152]{1,0:T(8,128)(2,1)S(1)}, bf16[192,1152]{1,0:T(8,128)(2,1)}, u32[]{:S(2)}) copy-start(bf16[192,1152]{1,0:T(8,128)(2,1)} %copy-done.7) | copy-start | bytes 1327108
  146.9 27.8 %copy-start.11 = (bf16[192,1152]{1,0:T(8,128)(2,1)S(1)}, bf16[192,1152]{1,0:T(8,128)(2,1)}, u32[]{:S(2)}) copy-start(bf16[192,1152]{1,0:T(8,128)(2,1)} %copy-done.9) | copy-start | bytes 1327108
  146.9 27.8 %copy-start.16 = (bf16[192,1152]{1,0:T(8,128)(2,1)S(1)}, bf16[192,1152]{1,0:T(8,128)(2,1)}, u32[]{:S(2)}) copy-start(bf16[192,1152]{1,0:T(8,128)(2,1)} %get-tuple-element.44.refs_13_.refs_12_) | copy-start | bytes 1327108
  146.9 27.8 %copy-start.18 = (bf16[192,1152]{1,0:T(8,128)(2,1)S(1)}, bf16[192,1152]{1,0:T(8,128)(2,1)}, u32[]{:S(2)}) copy-start(bf16[192,1152]{1,0:T(8,128)(2,1)} %copy-done.17) | copy-start | bytes 1327108
  147.0 53.9 %collective-permute-start.6 = (f32[192,1056]{1,0:T(8,128)}, f32[192,1056]{1,0:T(8,128)}, u32[]{:S(2)}, u32[]{:S(2)}) collective-permute-start(f32[192,1056]{1,0:T(8,128)} %copy-done.25), channel_id=1, source_target_pairs={{0,4},{4,8},{8,12},{12,16},{16,20},{20,24},{24,28},{1,5},{5,9},{9,... | collective-permute-start | bytes 2433032 | tf_op jit(solution)/shard_map/ppermute | solution.py:157
  174.7 0.9 copy-start.20
  184.0 26.7 %all-to-all-start.3 = ((f32[4,48,1024]{2,1,0:T(8,128)}), f32[4,48,1024]{2,1,0:T(8,128)}, u32[]{:S(2)}, u32[]{:S(2)}) async-start(f32[4,48,1024]{2,1,0:T(8,128)} %bitcast.101), calls=%async_computation.3 | async-start | bytes 1572864 | tf_op jit(solution)/shard_map/all_to_all | solution.py:187
  197.9 4.3 %copy-start.3 = (bf16[192,1152]{1,0:T(8,128)(2,1)S(1)}, bf16[192,1152]{1,0:T(8,128)(2,1)}, u32[]{:S(2)}) copy-start(bf16[192,1152]{1,0:T(8,128)(2,1)} %copy-done.1) | copy-start | bytes 1327108
  200.8 1.4 copy-start.6
  200.8 1.4 copy-start.13
  200.8 1.5 copy-start.15
  200.8 1.6 copy-start.19
  210.7 4.3 %copy-start.23 = (f32[48,64,64]{2,1,0:T(8,128)S(1)}, f32[48,64,64]{2,1,0:T(8,128)}, u32[]{:S(2)}) copy-start(f32[48,64,64]{2,1,0:T(8,128)} %reshape_broadcast_in_dim.13) | copy-start | bytes 2359300
  210.7 16.0 %all-to-all-start = ((f32[4,48,1024]{2,1,0:T(8,128)}), f32[4,48,1024]{2,1,0:T(8,128)}, u32[]{:S(2)}, u32[]{:S(2)}) async-start(f32[4,48,1024]{2,1,0:T(8,128)} %bitcast.103), calls=%async_computation | async-start | bytes 1572864 | tf_op jit(solution)/shard_map/all_to_all | solution.py:187
  215.1 3.5 %copy-start.24 = (f32[48,64,64]{2,1,0:T(8,128)S(1)}, f32[48,64,64]{2,1,0:T(8,128)}, u32[]{:S(2)}) copy-start(f32[48,64,64]{2,1,0:T(8,128)} %reshape_broadcast_in_dim.14) | copy-start | bytes 2359300
  215.1 3.5 %copy-start.31 = (f32[64,128,1]{1,0,2:T(8,128)S(1)}, f32[64,128,1]{1,0,2:T(8,128)}, u32[]{:S(2)}) copy-start(f32[64,128,1]{1,0,2:T(8,128)} %maximum_bitcast_fusion) | copy-start | bytes 98308
  252.1 4.2 %copy-start.22 = (f32[48,64,128]{2,1,0:T(8,128)S(1)}, f32[48,64,128]{2,1,0:T(8,128)}, u32[]{:S(2)}) copy-start(f32[48,64,128]{2,1,0:T(8,128)} %fusion.106) | copy-start | bytes 4718596
  252.1 4.2 %copy-start.33 = (f32[64,64]{1,0:T(8,128)S(1)}, f32[64,64]{1,0:T(8,128)}, u32[]{:S(2)}) copy-start(f32[64,64]{1,0:T(8,128)} %get-tuple-element.81) | copy-start | bytes 49156
  252.1 4.2 %copy-start.34 = (f32[64,64]{1,0:T(8,128)S(1)}, f32[64,64]{1,0:T(8,128)}, u32[]{:S(2)}) copy-start(f32[64,64]{1,0:T(8,128)} %get-tuple-element.82) | copy-start | bytes 49156
  280.2 0.9 copy-start.27
  280.2 1.1 copy-start.29
  280.2 1.2 copy-start.30
  281.4 1.7 copy-start.26
  281.4 1.7 copy-start.28
  (2 other events, 1.6 us)
